TPU v7x, 32 devices: a whole 2x2x4 slice. The times are simulated.
32 devices in a mesh: blk: 4 (over y, core), grp: 8 (over z, x).
Axes of the slice: x: 2, y: 2, z: 4, core: 2. Of those that a mesh axis runs over, the one named last changes fastest.
Arguments:
- features: bfloat16 [4096, 256], P(('blk', 'grp')), may hold values from -6 to 6
- weights: bfloat16 [2, 256, 256], replicated, may hold values from -0.375 to 0.375
- biases: float32 [2, 256], replicated, may hold values from -0.6 to 0.6
- adjacency: bfloat16 [4, 8, 6, 256, 256], P('blk', 'grp'), as said below
- tile_row: int32 [4, 8, 6], P('blk', 'grp'), may hold values from 0 to 1
- tile_column: int32 [4, 8, 6], P('blk', 'grp'), may hold values from 0 to 3
- tile_count: int32 [4, 8], P('blk', 'grp'), may hold values from 1 to 6, as said below
Outputs:
- result: bfloat16 [4096, 256], P(('blk', 'grp'))
Inputs may be any that keep to these rules, and one draw needn't show every extreme that they name: tile_count is at least 1 and at most 6; some device has exactly 6 live slots. `adjacency`: edge weights are zero or positive.
All inputs are finite; a program needn't handle non-finite values.
Results may differ from a plain program's by a relative error of at most 0.0046.
Values may be sent and summed in bfloat16 or wider, within the bound.
No kernel may reach another device: no remote copies, remote signals or barrier semaphores. Data moves between devices by JAX's collectives and lax.ppermute only.
A program may use at most 64 MiB of HBM per device.

v0:
```python
import jax
import jax.numpy as jnp
from jax import lax
from jax.sharding import PartitionSpec as P

LAYERS = 2


def aggregate(adjacency, cols_here, placing, column_rows, row_tiles):
    tile_size = adjacency.shape[1]
    width = column_rows.shape[1]
    blocks = column_rows.reshape(-1, tile_size, width)[cols_here]
    product = jnp.einsum("tij,tjf->tif", adjacency, blocks, preferred_element_type=jnp.float32)
    placed = jnp.einsum("rt,tif->rif", placing, product, precision=lax.Precision.HIGHEST)
    return placed.reshape(row_tiles * tile_size, width)


def on_device(features, weights, biases, adjacency, tile_row, tile_column, tile_count):
    adjacency = adjacency[0, 0]
    rows_here = tile_row[0, 0]
    cols_here = tile_column[0, 0]
    count_here = tile_count[0, 0]
    blk_size = lax.axis_size("blk")
    node_dev = features.shape[0]
    tile_size = adjacency.shape[1]
    slots = adjacency.shape[0]
    width = features.shape[1]
    row_tiles = blk_size * node_dev // tile_size
    live = lax.iota(jnp.int32, slots) < count_here
    placing = (
        (rows_here[None, :] == lax.iota(jnp.int32, row_tiles)[:, None]) & live[None, :]
    ).astype(jnp.float32)
    row_sums = jnp.sum(adjacency, axis=2, dtype=jnp.float32)
    degree_part = jnp.dot(placing, row_sums, precision=lax.Precision.HIGHEST).reshape(
        blk_size, node_dev
    )
    degree = lax.psum_scatter(degree_part, "blk", scatter_dimension=0, tiled=True)[0]
    scale = lax.rsqrt(1.0 + degree)[:, None]
    hidden = features
    result = None
    for layer_index in range(LAYERS):
        mixed = jnp.dot(hidden, weights[layer_index], preferred_element_type=jnp.float32)
        scaled = (mixed * scale).astype(jnp.bfloat16)
        column_rows = lax.all_gather(scaled, "grp", axis=0, tiled=True)
        partial_value = aggregate(adjacency, cols_here, placing, column_rows, row_tiles)
        partial_value = partial_value.reshape(blk_size, node_dev, width)
        summed = lax.psum_scatter(partial_value, "blk", scatter_dimension=0, tiled=True)[0]
        pre = (summed + scaled.astype(jnp.float32)) * scale + biases[layer_index][None, :]
        if layer_index < LAYERS - 1:
            hidden = jnp.maximum(pre, 0.0).astype(jnp.bfloat16)
        else:
            result = pre.astype(jnp.bfloat16)
    return result


def solution(mesh):
    placed = (
        P(("blk", "grp"), None),
        P(),
        P(),
        P("blk", "grp", None, None, None),
        P("blk", "grp", None),
        P("blk", "grp", None),
        P("blk", "grp"),
    )
    return jax.shard_map(
        on_device, mesh=mesh, in_specs=placed, out_specs=P(("blk", "grp"), None), check_vma=False
    )
```

profile of v0, /device:TPU:0, one launch (start us, length us, event | category | flops | bytes accessed | tf_op | source)
XLA Modules:
  0.0 150.4 jit_solution(8604493189462942408)
XLA Ops:
  7.3 1.4 convert_reduce_fusion
  8.7 0.8 fusion.31
  9.5 8.4 %all-reduce = f32[4,128]{1,0:T(4,128)S(1)} all-reduce(f32[4,128]{1,0:T(4,128)S(1)} %reshape.51), channel_id=2, replica_groups=mesh['blk'=4,'grp'=8] {'blk'}, use_global_device_ids=true, to_apply=%region_1.0.clone | all-reduce | flops 512 | bytes 4096
  17.9 1.2 dynamic-slice
  19.1 0.7 fusion.29
  19.8 1.1 fusion.4
  20.8 31.9 %all_gather.6 = bf16[1024,256]{1,0:T(8,128)(2,1)S(1)} all-gather(bf16[128,256]{1,0:T(8,128)(2,1)S(1)} %fusion.4), channel_id=1, replica_groups=mesh['blk'=4,'grp'=8] {'grp'}, dimensions={0}, use_global_device_ids=true | all-gather | bytes 589824 | tf_op jit(solution)/shard_map/all_gather | solution.py:44
  52.7 0.7 fusion.27
  53.4 0.6 gather_fusion
  54.0 1.6 %fusion.8 = f32[6,256,256]{2,1,0:T(8,128)} fusion(bf16[6,256,256]{2,1,0:T(8,128)(2,1)S(1)} %gather_fusion, bf16[1,1,6,256,256]{4,3,2,1,0:T(8,128)(2,1)S(1)} %copy-done.1), kind=kOutput, calls=%fused_computation.13 | convolution fusion | flops 201326592 | bytes 3145728 | tf_op jit(solution)/shard_map/tij,tjf->tif/dot_general | solution.py:13
  55.6 2.1 %copy.12 = f32[6,256,256]{1,0,2:T(8,128)S(1)} copy(f32[6,256,256]{2,1,0:T(8,128)} %fusion.8) | data formatting | bytes 3145728 | tf_op jit(solution)/shard_map/tij,tjf->tif/dot_general | solution.py:13
  57.7 1.1 fusion.2
  58.8 0.8 copy.10
  59.7 0.0 reduce-scatter.5.cloned.1.call-start
  59.7 21.6 %reduce-scatter.3.cloned.1.call-done = f32[1,128,256]{2,1,0:T(8,128)} async-done(((f32[4,128,256]{2,1,0:T(8,128)}), f32[1,128,256]{2,1,0:T(8,128)}) %reduce-scatter.3.cloned.1.call-update) | async-done | bytes 131088 | tf_op jit(solution)/shard_map/reduce_scatter | solution.py:47
  81.4 1.1 fusion.5
  82.5 31.3 %all_gather.7 = bf16[1024,256]{1,0:T(8,128)(2,1)S(1)} all-gather(bf16[128,256]{1,0:T(8,128)(2,1)S(1)} %fusion.5), channel_id=1, replica_groups=mesh['blk'=4,'grp'=8] {'grp'}, dimensions={0}, use_global_device_ids=true | all-gather | bytes 589824 | tf_op jit(solution)/shard_map/all_gather | solution.py:44
  113.8 0.6 gather_fusion.1
  114.4 1.6 %fusion.6 = f32[6,256,256]{2,1,0:T(8,128)} fusion(bf16[6,256,256]{2,1,0:T(8,128)(2,1)S(1)} %gather_fusion.1, bf16[1,1,6,256,256]{4,3,2,1,0:T(8,128)(2,1)S(1)} %copy-done.1), kind=kOutput, calls=%fused_computation.11 | convolution fusion | flops 201326592 | bytes 3145728 | tf_op jit(solution)/shard_map/tij,tjf->tif/dot_general | solution.py:13
  116.0 2.1 %copy.13 = f32[6,256,256]{1,0,2:T(8,128)S(1)} copy(f32[6,256,256]{2,1,0:T(8,128)} %fusion.6) | data formatting | bytes 3145728 | tf_op jit(solution)/shard_map/tij,tjf->tif/dot_general | solution.py:13
  118.1 1.1 fusion
  119.2 0.8 copy.11
  120.0 21.9 %reduce-scatter.5.cloned.1.call-done = f32[1,128,256]{2,1,0:T(8,128)} async-done(((f32[4,128,256]{2,1,0:T(8,128)}), f32[1,128,256]{2,1,0:T(8,128)}) %reduce-scatter.5.cloned.1.call-update) | async-done | bytes 131088 | tf_op jit(solution)/shard_map/reduce_scatter | solution.py:47
  141.9 1.6 %fusion.12 = bf16[128,256]{1,0:T(8,128)(2,1)} fusion(f32[1,128,256]{2,1,0:T(8,128)} %reduce-scatter.5.cloned.1.call-done, bf16[128,256]{1,0:T(8,128)(2,1)S(1)} %fusion.5, f32[256]{0:T(256)S(1)} %bitcast.69, f32[128]{0:T(128)S(1)} %fusion.29), kind=kLoop, calls=%fused_computation.18 | loop fusion | flops 163840 | bytes 263680 | tf_op jit(solution)/shard_map/convert_element_type | solution.py:52
  (17 shorter events, 0.1 us)
Async XLA Ops:
  6.5 13.2 %copy-start = (bf16[128,256]{1,0:T(8,128)(2,1)S(1)}, bf16[128,256]{1,0:T(8,128)(2,1)}, u32[]{:S(2)}) copy-start(bf16[128,256]{1,0:T(8,128)(2,1)} %param.7) | copy-start | bytes 196612
  6.5 47.4 %copy-start.1 = (bf16[1,1,6,256,256]{4,3,2,1,0:T(8,128)(2,1)S(1)}, bf16[1,1,6,256,256]{4,3,2,1,0:T(8,128)(2,1)}, u32[]{:S(2)}) copy-start(bf16[1,1,6,256,256]{4,3,2,1,0:T(8,128)(2,1)} %param.10) | copy-start | bytes 2359300
  6.5 74.8 %reduce-scatter.3.cloned.1.call-start = ((), (), s32[]{:S(2)}) async-start(), calls=%async_computation.2 | async-start | bytes 655360 | tf_op jit(solution)/shard_map/reduce_scatter | solution.py:47
  55.6 2.1 %copy-start.3 = (s32[1,1,6]{2,1,0:T(1,128)S(1)}, s32[1,1,6]{2,1,0:T(1,128)}, u32[]{:S(2)}) copy-start(s32[1,1,6]{2,1,0:T(1,128)} %param.11) | copy-start | bytes 76
  57.7 2.0 %copy-start.4 = (f32[2,256]{1,0:T(2,128)S(1)}, f32[2,256]{1,0:T(2,128)}, u32[]{:S(2)}) copy-start(f32[2,256]{1,0:T(2,128)} %param.9) | copy-start | bytes 6148
  57.7 23.6 %copy-start.2 = (bf16[2,256,256]{2,1,0:T(8,128)(2,1)S(1)}, bf16[2,256,256]{2,1,0:T(8,128)(2,1)}, u32[]{:S(2)}) copy-start(bf16[2,256,256]{2,1,0:T(8,128)(2,1)} %param.8) | copy-start | bytes 786436
  59.7 82.3 %reduce-scatter.5.cloned.1.call-start = ((), (), s32[]{:S(2)}) async-start(), calls=%async_computation.3 | async-start | bytes 655360 | tf_op jit(solution)/shard_map/reduce_scatter | solution.py:47
Sparse Core Ops, SparseCore 0:
  59.8 21.5 reduce-scatter.2
  120.1 21.7 reduce-scatter.4
where the time goes:
time: 151 us; the launch traced here: 150 us
  blocking collectives  71.6 us (47%)
  waiting for transfers between devices  43.6 us (29%)
  between operations  14.3 us (9%)
  local copies, waits for them, and re-layouts  8.33 us (6%)
  matrix products  8.28 us (5%)
  other arithmetic  4.35 us (3%)
    all_gather x2, blocking collectives, on_device(): column_rows = lax.all_gather(scaled, 'grp', axis=0, tiled=True)  63.2 us
    reduce_scatter x2, waiting for transfers between devices, on_device(): lax.psum_scatter(partial_value, 'blk', scatter_dimension=0, tiled=True)[0]  43.5 us
    unnamed x1, blocking collectives  8.36 us
    dot_general x2, local copies, waits for them, and re-layouts, aggregate(): jnp.einsum('tij,tjf->tif', adjacency, blocks, preferred_element_type=jnp....  4.21 us
    dot_general x2, matrix products, aggregate(): jnp.einsum('tij,tjf->tif', adjacency, blocks, preferred_element_type=jnp....  3.17 us
  transfers between devices with their start and end apart: 2, of which 2 were waited for; matrix products, arithmetic and copies ran while one was open for 0% of the time, Pallas kernels for 0%

commit v1 on v0

--- a/solution.py
+++ b/solution.py
@@ -4,6 +4,28 @@
 from jax.sharding import PartitionSpec as P
 
 LAYERS = 2
+
+
+def laid_out(blocks, dim):
+    blocks = jnp.moveaxis(blocks, 0, dim)
+    shape = blocks.shape
+    return blocks.reshape(*shape[:dim], shape[dim] * shape[dim + 1], *shape[dim + 2 :])
+
+
+def collect(x, axis, dim):
+    length = lax.axis_size(axis)
+    pairs = [(i, (i + 1) % length) for i in range(length)]
+    back = [(b, a) for a, b in pairs]
+    lower, upper = ([], [])
+    for hop in range(length - 1):
+        if hop % 2 == 0:
+            lower.append(lax.ppermute(lower[-1] if lower else x, axis, pairs))
+        else:
+            upper.append(lax.ppermute(upper[-1] if upper else x, axis, back))
+    parts = jnp.stack([*lower[::-1], x, *upper])
+    shift = lax.axis_index(axis) - len(lower)
+    parts = parts[(jnp.arange(length) - shift) % length]
+    return laid_out(parts, dim)
 
 
 def aggregate(adjacency, cols_here, placing, column_rows, row_tiles):
@@ -41,7 +63,7 @@
     for layer_index in range(LAYERS):
         mixed = jnp.dot(hidden, weights[layer_index], preferred_element_type=jnp.float32)
         scaled = (mixed * scale).astype(jnp.bfloat16)
-        column_rows = lax.all_gather(scaled, "grp", axis=0, tiled=True)
+        column_rows = collect(scaled, "grp", 0)
         partial_value = aggregate(adjacency, cols_here, placing, column_rows, row_tiles)
         partial_value = partial_value.reshape(blk_size, node_dev, width)
         summed = lax.psum_scatter(partial_value, "blk", scatter_dimension=0, tiled=True)[0]

time: 151 us -> 145 us (0.960)
  blocking collectives: 71.6 us -> 8.36 us
  starting transfers between devices: 0.04 us -> 30.1 us
  waiting for transfers between devices: 43.6 us -> 69.7 us
    all_gather x2 -> x0, blocking collectives: 63.2 us -> none  [on_device(): column_rows = lax.all_gather(scaled, 'grp', axis=0, tiled=True)]
    ppermute x0 -> x14, starting transfers between devices: none -> 30 us  [the longest x6 26.9 us: collect(): upper.append(lax.ppermute(upper[-1] if upper else x, axis, back))]
    ppermute x0 -> x14, waiting for transfers between devices: none -> 25.3 us  [the longest x8 25.3 us: collect(): lower.append(lax.ppermute(lower[-1] if lower else x, axis, pairs))]
  transfers between devices with their start and end apart: 2 -> 16, of which waited for: 2 -> 10; matrix products, arithmetic and copies ran while one was open for 0% -> 1% of each run, Pallas kernels for 0% -> 0%
where the time goes in v1:
time: 145 us
  waiting for transfers between devices  69.7 us (48%)
  starting transfers between devices  30.1 us (21%)
  between operations  14.4 us (10%)
  local copies, waits for them, and re-layouts  9.61 us (7%)
  matrix products  8.38 us (6%)
  blocking collectives  8.36 us (6%)
  other arithmetic  4.37 us (3%)
    reduce_scatter x2, waiting for transfers between devices, on_device(): lax.psum_scatter(partial_value, 'blk', scatter_dimension=0, tiled=True)[0]  44.3 us
    ppermute x6, starting transfers between devices, collect(): upper.append(lax.ppermute(upper[-1] if upper else x, axis, back))  26.9 us
    ppermute x8, waiting for transfers between devices, collect(): lower.append(lax.ppermute(lower[-1] if lower else x, axis, pairs))  25.3 us
    unnamed x1, blocking collectives  8.36 us
    dot_general x2, local copies, waits for them, and re-layouts, aggregate(): jnp.einsum('tij,tjf->tif', adjacency, blocks, preferred_element_type=jnp....  4.21 us
    dot_general x2, matrix products, aggregate(): jnp.einsum('tij,tjf->tif', adjacency, blocks, preferred_element_type=jnp....  3.19 us
    ppermute x8, starting transfers between devices, collect(): lower.append(lax.ppermute(lower[-1] if lower else x, axis, pairs))  3.09 us
  transfers between devices with their start and end apart: 16, of which 10 were waited for; matrix products, arithmetic and copies ran while one was open for 1% of the time, Pallas kernels for 0%

profile of v1, /device:TPU:0, one launch (start us, length us, event | category | flops | bytes accessed | tf_op | source)
XLA Modules:
  0.0 144.8 jit_solution(653108213674877496)
XLA Ops:
  9.5 8.4 %all-reduce = f32[4,128]{1,0:T(4,128)S(1)} all-reduce(f32[4,128]{1,0:T(4,128)S(1)} %reshape.94), channel_id=2, replica_groups=mesh['blk'=4,'grp'=8] {'blk'}, use_global_device_ids=true, to_apply=%region_1.0.clone | all-reduce | flops 512 | bytes 4096
  20.9 1.5 %collective-permute-start = (bf16[128,256]{1,0:T(8,128)(2,1)S(1)}, bf16[128,256]{1,0:T(8,128)(2,1)S(1)}, u32[]{:S(2)}, u32[]{:S(2)}) collective-permute-start(bf16[128,256]{1,0:T(8,128)(2,1)S(1)} %fusion.4), channel_id=1, source_target_pairs={{0,1},{1,2},{2,3},{3,4},{4,5},{5,6},{6,7},{7,0},{8,9},{9,10},{10,1... | collective-permute-start | bytes 196616 | tf_op jit(solution)/shard_map/ppermute | solution.py:22
  22.4 3.2 %collective-permute-start.4 = (bf16[128,256]{1,0:T(8,128)(2,1)S(1)}, bf16[128,256]{1,0:T(8,128)(2,1)S(1)}, u32[]{:S(2)}, u32[]{:S(2)}) collective-permute-start(bf16[128,256]{1,0:T(8,128)(2,1)S(1)} %fusion.4), channel_id=1, source_target_pairs={{1,0},{2,1},{3,2},{4,3},{5,4},{6,5},{7,6},{0,7},{9,8},{10,9},{11,1... | collective-permute-start | bytes 196616 | tf_op jit(solution)/shard_map/ppermute | solution.py:24
  26.3 1.6 %collective-permute-done = bf16[128,256]{1,0:T(8,128)(2,1)S(1)} collective-permute-done((bf16[128,256]{1,0:T(8,128)(2,1)S(1)}, bf16[128,256]{1,0:T(8,128)(2,1)S(1)}, u32[]{:S(2)}, u32[]{:S(2)}) %collective-permute-start) | collective-permute-done | bytes 65568 | tf_op jit(solution)/shard_map/ppermute | solution.py:22
  27.9 7.1 %collective-permute-done.1 = bf16[128,256]{1,0:T(8,128)(2,1)S(1)} collective-permute-done((bf16[128,256]{1,0:T(8,128)(2,1)S(1)}, bf16[128,256]{1,0:T(8,128)(2,1)S(1)}, u32[]{:S(2)}, u32[]{:S(2)}) %collective-permute-start.1) | collective-permute-done | bytes 65568 | tf_op jit(solution)/shard_map/ppermute | solution.py:22
  35.0 4.8 %collective-permute-start.5 = (bf16[128,256]{1,0:T(8,128)(2,1)S(1)}, bf16[128,256]{1,0:T(8,128)(2,1)S(1)}, u32[]{:S(2)}, u32[]{:S(2)}) collective-permute-start(bf16[128,256]{1,0:T(8,128)(2,1)S(1)} %collective-permute-done.4), channel_id=1, source_target_pairs={{1,0},{2,1},{3,2},{4,3},{5,4},{6,5},{7,6},{0,7},{9,8},{10,9},{11,1... | collective-permute-start | bytes 196616 | tf_op jit(solution)/shard_map/ppermute | solution.py:24
  39.7 2.2 %collective-permute-done.2 = bf16[128,256]{1,0:T(8,128)(2,1)S(1)} collective-permute-done((bf16[128,256]{1,0:T(8,128)(2,1)S(1)}, bf16[128,256]{1,0:T(8,128)(2,1)S(1)}, u32[]{:S(2)}, u32[]{:S(2)}) %collective-permute-start.2) | collective-permute-done | bytes 65568 | tf_op jit(solution)/shard_map/ppermute | solution.py:22
  41.9 4.8 %collective-permute-start.6 = (bf16[128,256]{1,0:T(8,128)(2,1)S(1)}, bf16[128,256]{1,0:T(8,128)(2,1)S(1)}, u32[]{:S(2)}, u32[]{:S(2)}) collective-permute-start(bf16[128,256]{1,0:T(8,128)(2,1)S(1)} %collective-permute-done.5), channel_id=1, source_target_pairs={{1,0},{2,1},{3,2},{4,3},{5,4},{6,5},{7,6},{0,7},{9,8},{10,9},{11,1... | collective-permute-start | bytes 196616 | tf_op jit(solution)/shard_map/ppermute | solution.py:24
  46.7 2.2 %collective-permute-done.3 = bf16[128,256]{1,0:T(8,128)(2,1)S(1)} collective-permute-done((bf16[128,256]{1,0:T(8,128)(2,1)S(1)}, bf16[128,256]{1,0:T(8,128)(2,1)S(1)}, u32[]{:S(2)}, u32[]{:S(2)}) %collective-permute-start.3) | collective-permute-done | bytes 65568 | tf_op jit(solution)/shard_map/ppermute | solution.py:22
  50.2 1.6 %fusion.8 = f32[6,256,256]{2,1,0:T(8,128)} fusion(bf16[6,256,256]{2,1,0:T(8,128)(2,1)S(1)} %gather_fusion.1, bf16[1,1,6,256,256]{4,3,2,1,0:T(8,128)(2,1)S(1)} %copy-done.1), kind=kOutput, calls=%fused_computation.15 | convolution fusion | flops 201326592 | bytes 3145728 | tf_op jit(solution)/shard_map/tij,tjf->tif/dot_general | solution.py:35
  51.8 2.1 %copy.12 = f32[6,256,256]{1,0,2:T(8,128)S(1)} copy(f32[6,256,256]{2,1,0:T(8,128)} %fusion.8) | data formatting | bytes 3145728 | tf_op jit(solution)/shard_map/tij,tjf->tif/dot_general | solution.py:35
  56.0 22.2 %reduce-scatter.3.cloned.1.call-done = f32[1,128,256]{2,1,0:T(8,128)} async-done(((f32[4,128,256]{2,1,0:T(8,128)}), f32[1,128,256]{2,1,0:T(8,128)}) %reduce-scatter.3.cloned.1.call-update) | async-done | bytes 131088 | tf_op jit(solution)/shard_map/reduce_scatter | solution.py:69
  79.3 1.5 %collective-permute-start.7 = (bf16[128,256]{1,0:T(8,128)(2,1)S(1)}, bf16[128,256]{1,0:T(8,128)(2,1)S(1)}, u32[]{:S(2)}, u32[]{:S(2)}) collective-permute-start(bf16[128,256]{1,0:T(8,128)(2,1)S(1)} %fusion.5), channel_id=1, source_target_pairs={{0,1},{1,2},{2,3},{3,4},{4,5},{5,6},{6,7},{7,0},{8,9},{9,10},{10,1... | collective-permute-start | bytes 196616 | tf_op jit(solution)/shard_map/ppermute | solution.py:22
  80.8 5.5 %collective-permute-done.7 = bf16[128,256]{1,0:T(8,128)(2,1)S(1)} collective-permute-done((bf16[128,256]{1,0:T(8,128)(2,1)S(1)}, bf16[128,256]{1,0:T(8,128)(2,1)S(1)}, u32[]{:S(2)}, u32[]{:S(2)}) %collective-permute-start.7) | collective-permute-done | bytes 65568 | tf_op jit(solution)/shard_map/ppermute | solution.py:22
  86.3 4.7 %collective-permute-start.11 = (bf16[128,256]{1,0:T(8,128)(2,1)S(1)}, bf16[128,256]{1,0:T(8,128)(2,1)S(1)}, u32[]{:S(2)}, u32[]{:S(2)}) collective-permute-start(bf16[128,256]{1,0:T(8,128)(2,1)S(1)} %fusion.5), channel_id=1, source_target_pairs={{1,0},{2,1},{3,2},{4,3},{5,4},{6,5},{7,6},{0,7},{9,8},{10,9},{11,1... | collective-permute-start | bytes 196616 | tf_op jit(solution)/shard_map/ppermute | solution.py:24
  91.0 2.2 %collective-permute-done.8 = bf16[128,256]{1,0:T(8,128)(2,1)S(1)} collective-permute-done((bf16[128,256]{1,0:T(8,128)(2,1)S(1)}, bf16[128,256]{1,0:T(8,128)(2,1)S(1)}, u32[]{:S(2)}, u32[]{:S(2)}) %collective-permute-start.8) | collective-permute-done | bytes 65568 | tf_op jit(solution)/shard_map/ppermute | solution.py:22
  93.2 4.7 %collective-permute-start.12 = (bf16[128,256]{1,0:T(8,128)(2,1)S(1)}, bf16[128,256]{1,0:T(8,128)(2,1)S(1)}, u32[]{:S(2)}, u32[]{:S(2)}) collective-permute-start(bf16[128,256]{1,0:T(8,128)(2,1)S(1)} %collective-permute-done.11), channel_id=1, source_target_pairs={{1,0},{2,1},{3,2},{4,3},{5,4},{6,5},{7,6},{0,7},{9,8},{10,9},{11,1... | collective-permute-start | bytes 196616 | tf_op jit(solution)/shard_map/ppermute | solution.py:24
  98.0 2.3 %collective-permute-done.9 = bf16[128,256]{1,0:T(8,128)(2,1)S(1)} collective-permute-done((bf16[128,256]{1,0:T(8,128)(2,1)S(1)}, bf16[128,256]{1,0:T(8,128)(2,1)S(1)}, u32[]{:S(2)}, u32[]{:S(2)}) %collective-permute-start.9) | collective-permute-done | bytes 65568 | tf_op jit(solution)/shard_map/ppermute | solution.py:22
  100.3 4.7 %collective-permute-start.13 = (bf16[128,256]{1,0:T(8,128)(2,1)S(1)}, bf16[128,256]{1,0:T(8,128)(2,1)S(1)}, u32[]{:S(2)}, u32[]{:S(2)}) collective-permute-start(bf16[128,256]{1,0:T(8,128)(2,1)S(1)} %collective-permute-done.12), channel_id=1, source_target_pairs={{1,0},{2,1},{3,2},{4,3},{5,4},{6,5},{7,6},{0,7},{9,8},{10,9},{11,1... | collective-permute-start | bytes 196616 | tf_op jit(solution)/shard_map/ppermute | solution.py:24
  105.0 2.2 %collective-permute-done.10 = bf16[128,256]{1,0:T(8,128)(2,1)S(1)} collective-permute-done((bf16[128,256]{1,0:T(8,128)(2,1)S(1)}, bf16[128,256]{1,0:T(8,128)(2,1)S(1)}, u32[]{:S(2)}, u32[]{:S(2)}) %collective-permute-start.10) | collective-permute-done | bytes 65568 | tf_op jit(solution)/shard_map/ppermute | solution.py:22
  108.6 1.6 %fusion.6 = f32[6,256,256]{2,1,0:T(8,128)} fusion(bf16[6,256,256]{2,1,0:T(8,128)(2,1)S(1)} %gather_fusion.3, bf16[1,1,6,256,256]{4,3,2,1,0:T(8,128)(2,1)S(1)} %copy-done.1), kind=kOutput, calls=%fused_computation.13 | convolution fusion | flops 201326592 | bytes 3145728 | tf_op jit(solution)/shard_map/tij,tjf->tif/dot_general | solution.py:35
  110.2 2.1 %copy.13 = f32[6,256,256]{1,0,2:T(8,128)S(1)} copy(f32[6,256,256]{2,1,0:T(8,128)} %fusion.6) | data formatting | bytes 3145728 | tf_op jit(solution)/shard_map/tij,tjf->tif/dot_general | solution.py:35
  114.2 22.2 %reduce-scatter.5.cloned.1.call-done = f32[1,128,256]{2,1,0:T(8,128)} async-done(((f32[4,128,256]{2,1,0:T(8,128)}), f32[1,128,256]{2,1,0:T(8,128)}) %reduce-scatter.5.cloned.1.call-update) | async-done | bytes 131088 | tf_op jit(solution)/shard_map/reduce_scatter | solution.py:69
  136.4 1.6 %fusion.12 = bf16[128,256]{1,0:T(8,128)(2,1)} fusion(f32[1,128,256]{2,1,0:T(8,128)} %reduce-scatter.5.cloned.1.call-done, bf16[128,256]{1,0:T(8,128)(2,1)S(1)} %fusion.5, f32[256]{0:T(256)S(1)} %bitcast.103, f32[128]{0:T(128)S(1)} %fusion.31), kind=kLoop, calls=%fused_computation.20 | loop fusion | flops 163840 | bytes 263680 | tf_op jit(solution)/shard_map/convert_element_type | solution.py:74
  (63 shorter events, 13.4 us)
Async XLA Ops:
  6.5 13.3 %copy-start = (bf16[128,256]{1,0:T(8,128)(2,1)S(1)}, bf16[128,256]{1,0:T(8,128)(2,1)}, u32[]{:S(2)}) copy-start(bf16[128,256]{1,0:T(8,128)(2,1)} %param.7) | copy-start | bytes 196612
  6.5 71.6 %reduce-scatter.3.cloned.1.call-start = ((), (), s32[]{:S(2)}) async-start(), calls=%async_computation.2 | async-start | bytes 655360 | tf_op jit(solution)/shard_map/reduce_scatter | solution.py:69
  8.7 41.5 %copy-start.1 = (bf16[1,1,6,256,256]{4,3,2,1,0:T(8,128)(2,1)S(1)}, bf16[1,1,6,256,256]{4,3,2,1,0:T(8,128)(2,1)}, u32[]{:S(2)}) copy-start(bf16[1,1,6,256,256]{4,3,2,1,0:T(8,128)(2,1)} %param.10) | copy-start | bytes 2359300
  20.9 7.0 %collective-permute-start = (bf16[128,256]{1,0:T(8,128)(2,1)S(1)}, bf16[128,256]{1,0:T(8,128)(2,1)S(1)}, u32[]{:S(2)}, u32[]{:S(2)}) collective-permute-start(bf16[128,256]{1,0:T(8,128)(2,1)S(1)} %fusion.4), channel_id=1, source_target_pairs={{0,1},{1,2},{2,3},{3,4},{4,5},{5,6},{6,7},{7,0},{8,9},{9,10},{10,1... | collective-permute-start | bytes 196616 | tf_op jit(solution)/shard_map/ppermute | solution.py:22
  22.4 12.6 %collective-permute-start.4 = (bf16[128,256]{1,0:T(8,128)(2,1)S(1)}, bf16[128,256]{1,0:T(8,128)(2,1)S(1)}, u32[]{:S(2)}, u32[]{:S(2)}) collective-permute-start(bf16[128,256]{1,0:T(8,128)(2,1)S(1)} %fusion.4), channel_id=1, source_target_pairs={{1,0},{2,1},{3,2},{4,3},{5,4},{6,5},{7,6},{0,7},{9,8},{10,9},{11,1... | collective-permute-start | bytes 196616 | tf_op jit(solution)/shard_map/ppermute | solution.py:24
  27.9 7.1 %collective-permute-start.1 = (bf16[128,256]{1,0:T(8,128)(2,1)S(1)}, bf16[128,256]{1,0:T(8,128)(2,1)S(1)}, u32[]{:S(2)}, u32[]{:S(2)}) collective-permute-start(bf16[128,256]{1,0:T(8,128)(2,1)S(1)} %collective-permute-done), channel_id=1, source_target_pairs={{0,1},{1,2},{2,3},{3,4},{4,5},{5,6},{6,7},{7,0},{8,9},{9,10},{10,1... | collective-permute-start | bytes 196616 | tf_op jit(solution)/shard_map/ppermute | solution.py:22
  35.0 7.0 %collective-permute-start.2 = (bf16[128,256]{1,0:T(8,128)(2,1)S(1)}, bf16[128,256]{1,0:T(8,128)(2,1)S(1)}, u32[]{:S(2)}, u32[]{:S(2)}) collective-permute-start(bf16[128,256]{1,0:T(8,128)(2,1)S(1)} %collective-permute-done.1), channel_id=1, source_target_pairs={{0,1},{1,2},{2,3},{3,4},{4,5},{5,6},{6,7},{7,0},{8,9},{9,10},{10,1... | collective-permute-start | bytes 196616 | tf_op jit(solution)/shard_map/ppermute | solution.py:22
  35.0 7.0 %collective-permute-start.5 = (bf16[128,256]{1,0:T(8,128)(2,1)S(1)}, bf16[128,256]{1,0:T(8,128)(2,1)S(1)}, u32[]{:S(2)}, u32[]{:S(2)}) collective-permute-start(bf16[128,256]{1,0:T(8,128)(2,1)S(1)} %collective-permute-done.4), channel_id=1, source_target_pairs={{1,0},{2,1},{3,2},{4,3},{5,4},{6,5},{7,6},{0,7},{9,8},{10,9},{11,1... | collective-permute-start | bytes 196616 | tf_op jit(solution)/shard_map/ppermute | solution.py:24
  41.9 7.0 %collective-permute-start.3 = (bf16[128,256]{1,0:T(8,128)(2,1)S(1)}, bf16[128,256]{1,0:T(8,128)(2,1)S(1)}, u32[]{:S(2)}, u32[]{:S(2)}) collective-permute-start(bf16[128,256]{1,0:T(8,128)(2,1)S(1)} %collective-permute-done.2), channel_id=1, source_target_pairs={{0,1},{1,2},{2,3},{3,4},{4,5},{5,6},{6,7},{7,0},{8,9},{9,10},{10,1... | collective-permute-start | bytes 196616 | tf_op jit(solution)/shard_map/ppermute | solution.py:22
  41.9 7.0 %collective-permute-start.6 = (bf16[128,256]{1,0:T(8,128)(2,1)S(1)}, bf16[128,256]{1,0:T(8,128)(2,1)S(1)}, u32[]{:S(2)}, u32[]{:S(2)}) collective-permute-start(bf16[128,256]{1,0:T(8,128)(2,1)S(1)} %collective-permute-done.5), channel_id=1, source_target_pairs={{1,0},{2,1},{3,2},{4,3},{5,4},{6,5},{7,6},{0,7},{9,8},{10,9},{11,1... | collective-permute-start | bytes 196616 | tf_op jit(solution)/shard_map/ppermute | solution.py:24
  51.8 2.1 %copy-start.3 = (s32[1,1,6]{2,1,0:T(1,128)S(1)}, s32[1,1,6]{2,1,0:T(1,128)}, u32[]{:S(2)}) copy-start(s32[1,1,6]{2,1,0:T(1,128)} %param.11) | copy-start | bytes 76
  53.9 2.0 %copy-start.4 = (f32[2,256]{1,0:T(2,128)S(1)}, f32[2,256]{1,0:T(2,128)}, u32[]{:S(2)}) copy-start(f32[2,256]{1,0:T(2,128)} %param.9) | copy-start | bytes 6148
  53.9 24.2 %copy-start.2 = (bf16[2,256,256]{2,1,0:T(8,128)(2,1)S(1)}, bf16[2,256,256]{2,1,0:T(8,128)(2,1)}, u32[]{:S(2)}) copy-start(bf16[2,256,256]{2,1,0:T(8,128)(2,1)} %param.8) | copy-start | bytes 786436
  55.9 80.5 %reduce-scatter.5.cloned.1.call-start = ((), (), s32[]{:S(2)}) async-start(), calls=%async_computation.3 | async-start | bytes 655360 | tf_op jit(solution)/shard_map/reduce_scatter | solution.py:69
  79.3 7.0 %collective-permute-start.7 = (bf16[128,256]{1,0:T(8,128)(2,1)S(1)}, bf16[128,256]{1,0:T(8,128)(2,1)S(1)}, u32[]{:S(2)}, u32[]{:S(2)}) collective-permute-start(bf16[128,256]{1,0:T(8,128)(2,1)S(1)} %fusion.5), channel_id=1, source_target_pairs={{0,1},{1,2},{2,3},{3,4},{4,5},{5,6},{6,7},{7,0},{8,9},{9,10},{10,1... | collective-permute-start | bytes 196616 | tf_op jit(solution)/shard_map/ppermute | solution.py:22
  86.3 7.0 %collective-permute-start.8 = (bf16[128,256]{1,0:T(8,128)(2,1)S(1)}, bf16[128,256]{1,0:T(8,128)(2,1)S(1)}, u32[]{:S(2)}, u32[]{:S(2)}) collective-permute-start(bf16[128,256]{1,0:T(8,128)(2,1)S(1)} %collective-permute-done.7), channel_id=1, source_target_pairs={{0,1},{1,2},{2,3},{3,4},{4,5},{5,6},{6,7},{7,0},{8,9},{9,10},{10,1... | collective-permute-start | bytes 196616 | tf_op jit(solution)/shard_map/ppermute | solution.py:22
  86.3 7.0 %collective-permute-start.11 = (bf16[128,256]{1,0:T(8,128)(2,1)S(1)}, bf16[128,256]{1,0:T(8,128)(2,1)S(1)}, u32[]{:S(2)}, u32[]{:S(2)}) collective-permute-start(bf16[128,256]{1,0:T(8,128)(2,1)S(1)} %fusion.5), channel_id=1, source_target_pairs={{1,0},{2,1},{3,2},{4,3},{5,4},{6,5},{7,6},{0,7},{9,8},{10,9},{11,1... | collective-permute-start | bytes 196616 | tf_op jit(solution)/shard_map/ppermute | solution.py:24
  93.2 7.1 %collective-permute-start.9 = (bf16[128,256]{1,0:T(8,128)(2,1)S(1)}, bf16[128,256]{1,0:T(8,128)(2,1)S(1)}, u32[]{:S(2)}, u32[]{:S(2)}) collective-permute-start(bf16[128,256]{1,0:T(8,128)(2,1)S(1)} %collective-permute-done.8), channel_id=1, source_target_pairs={{0,1},{1,2},{2,3},{3,4},{4,5},{5,6},{6,7},{7,0},{8,9},{9,10},{10,1... | collective-permute-start | bytes 196616 | tf_op jit(solution)/shard_map/ppermute | solution.py:22
  93.2 7.1 %collective-permute-start.12 = (bf16[128,256]{1,0:T(8,128)(2,1)S(1)}, bf16[128,256]{1,0:T(8,128)(2,1)S(1)}, u32[]{:S(2)}, u32[]{:S(2)}) collective-permute-start(bf16[128,256]{1,0:T(8,128)(2,1)S(1)} %collective-permute-done.11), channel_id=1, source_target_pairs={{1,0},{2,1},{3,2},{4,3},{5,4},{6,5},{7,6},{0,7},{9,8},{10,9},{11,1... | collective-permute-start | bytes 196616 | tf_op jit(solution)/shard_map/ppermute | solution.py:24
  100.3 7.0 %collective-permute-start.10 = (bf16[128,256]{1,0:T(8,128)(2,1)S(1)}, bf16[128,256]{1,0:T(8,128)(2,1)S(1)}, u32[]{:S(2)}, u32[]{:S(2)}) collective-permute-start(bf16[128,256]{1,0:T(8,128)(2,1)S(1)} %collective-permute-done.9), channel_id=1, source_target_pairs={{0,1},{1,2},{2,3},{3,4},{4,5},{5,6},{6,7},{7,0},{8,9},{9,10},{10,1... | collective-permute-start | bytes 196616 | tf_op jit(solution)/shard_map/ppermute | solution.py:22
  100.3 7.0 %collective-permute-start.13 = (bf16[128,256]{1,0:T(8,128)(2,1)S(1)}, bf16[128,256]{1,0:T(8,128)(2,1)S(1)}, u32[]{:S(2)}, u32[]{:S(2)}) collective-permute-start(bf16[128,256]{1,0:T(8,128)(2,1)S(1)} %collective-permute-done.12), channel_id=1, source_target_pairs={{1,0},{2,1},{3,2},{4,3},{5,4},{6,5},{7,6},{0,7},{9,8},{10,9},{11,1... | collective-permute-start | bytes 196616 | tf_op jit(solution)/shard_map/ppermute | solution.py:24
Sparse Core Ops, SparseCore 0:
  56.0 22.0 reduce-scatter.2
  114.3 22.0 reduce-scatter.4
